TPU v7x, 512 devices: a whole 4x8x8 slice. The times are simulated.
512 devices in a mesh: grp: 16 (over z, core), tok: 32 (over y, x).
Axes of the slice: x: 4, y: 8, z: 8, core: 2. Of those that a mesh axis runs over, the one named last changes fastest.
Arguments:
- patches: bfloat16 [32, 256, 1664], P('tok', 'grp'), may hold values from -54 to 54
- segment_ids: int32 [32, 256], P('tok'), may hold values from 0 to 32, as said below
- padding: int32 [32, 256], P('tok'), may hold values from 0 to 1, as said below
- request_owner: int32 [32, 32], P('tok'), may hold values from 0 to 31, as said below
- first_gain: float32 [1664], replicated, may hold values from 0.5 to 1.5
- first_shift: float32 [1664], replicated, may hold values from -3 to 3
- input_weight: bfloat16 [1664, 16, 312], P(None, 'grp'), may hold values from -0.15625 to 0.15625
- input_shift: float32 [16, 312], P('grp'), may hold values from -40 to 40
- output_weight: bfloat16 [16, 104, 1664], P('grp'), may hold values from -0.15625 to 0.15625
- output_shift: float32 [1664], replicated, may hold values from -3 to 3
- second_gain: float32 [1664], replicated, may hold values from 0.5 to 1.5
- second_shift: float32 [1664], replicated, may hold values from -3 to 3
- up_weight: bfloat16 [1664, 4096], P(None, 'grp'), may hold values from -0.15625 to 0.15625
- up_shift: float32 [4096], P('grp'), may hold values from -3 to 3
- down_weight: bfloat16 [4096, 1664], P('grp'), may hold values from -0.09375 to 0.09375
- down_shift: float32 [1664], replicated, may hold values from -3 to 3
- merge_weight: bfloat16 [6656, 1664], P(None, 'grp'), may hold values from -0.078125 to 0.078125
- merge_shift: float32 [1664], P('grp'), may hold values from -3 to 3
Outputs:
- routed: bfloat16 [32, 32, 8, 1664], P('tok', None, None, 'grp')
Inputs may be any that keep to these rules, and one draw needn't show every extreme that they name: `segment_ids`: patches come in aligned runs of four with one id (a 2x2 window); ids never fall along a group; an image spans 1 to 8 windows; every group holds an image of exactly 8 windows; padding stands at the end of a group and carries the id 32. `padding`: 0 exactly where segment_ids is 32. `request_owner`: every row is a permutation of 0 to 31; in every draw one owner receives an image of 8 windows from every group.
All inputs are finite; a program needn't handle non-finite values.
Results may differ from a plain program's by a relative error of at most 0.02.
The roundings to bfloat16 on the way count: a program that leaves them out, or rounds other values in their place, can miss the bound.
Values may be sent and summed in bfloat16 or wider, within the bound.
No kernel may reach another device: no remote copies, remote signals or barrier semaphores. Data moves between devices by JAX's collectives and lax.ppermute only.
A program may use at most 64 MiB of HBM per device.

v0:
```python
import jax
import jax.numpy as jnp
from jax import lax
from jax.sharding import PartitionSpec as P

CAP = 8
epsilon = 1e-06


def normalize(stream, factor, adjust):
    average = jnp.mean(stream, axis=-1, keepdims=True)
    centered = stream - average
    variance = jnp.mean(centered * centered, axis=-1, keepdims=True)
    return centered * lax.rsqrt(variance + epsilon) * factor + adjust


def attention_mask(segments, live_rows):
    count = segments.shape[0]
    same_image = segments[:, None] == segments[None, :]
    allowed = jnp.logical_and(same_image, live_rows[None, :] == 1)
    diagonal = jnp.arange(count)[:, None] == jnp.arange(count)[None, :]
    return jnp.logical_or(allowed, diagonal)


def softmax_rows(scores, allowed):
    masked = jnp.where(allowed, scores, -jnp.inf)
    row_max = jnp.max(masked, axis=-1, keepdims=True)
    powered = jnp.where(allowed, jnp.exp(masked - row_max), 0.0)
    return powered / jnp.sum(powered, axis=-1, keepdims=True)


def attend(projected, segments, live_rows, head_dim):
    queries = projected[:, :, :head_dim]
    key_rows = projected[:, :, head_dim : 2 * head_dim]
    value_rows = projected[:, :, 2 * head_dim :]
    scores = jnp.einsum(
        "qhe,khe->hqk", queries, key_rows, preferred_element_type=jnp.float32
    ) * head_dim ** (-0.5)
    probabilities = lax.optimization_barrier(
        softmax_rows(scores, attention_mask(segments, live_rows)[None]).astype(jnp.bfloat16)
    )
    return jnp.einsum(
        "hqk,khe->qhe", probabilities, value_rows, preferred_element_type=jnp.float32
    ).astype(jnp.bfloat16)


def summed_apart(terms):
    shards = lax.psum(1, "grp")
    rows = terms.shape[0] // shards
    pieces = lax.all_to_all(terms.reshape(shards, rows, terms.shape[1]), "grp", 0, 0, tiled=False)
    return jnp.sum(pieces.astype(jnp.float32), axis=0)


def routed_rows(merged, segments, live_rows, owners):
    window_segments = segments[::4]
    window_live = live_rows[::4]
    window_count = window_segments.shape[0]
    places = jnp.arange(window_count)
    earlier = jnp.logical_and(
        window_segments[None, :] == window_segments[:, None], places[None, :] < places[:, None]
    )
    slot_index = jnp.sum(earlier.astype(jnp.int32), axis=1)
    groups = owners.shape[0]
    matched = (jnp.arange(groups)[None, :] == window_segments[:, None]).astype(jnp.int32)
    owner_of = jnp.sum(matched * owners[None, :], axis=1)
    target = owner_of * CAP + slot_index
    one_hot = jnp.logical_and(
        target[:, None] == jnp.arange(groups * CAP)[None, :], window_live[:, None] == 1
    )
    outgoing = jnp.einsum(
        "wc,wd->cd", one_hot.astype(jnp.bfloat16), merged, preferred_element_type=jnp.float32
    )
    return outgoing.astype(jnp.bfloat16).reshape(groups, CAP, merged.shape[1])


def on_device(
    patches,
    segment_ids,
    padding,
    request_owner,
    first_gain,
    first_shift,
    input_weight,
    input_shift,
    output_weight,
    output_shift,
    second_gain,
    second_shift,
    up_weight,
    up_shift,
    down_weight,
    down_shift,
    merge_weight,
    merge_shift,
):
    row_count = patches.shape[1]
    model_width = patches.shape[2]
    head_dim = input_weight.shape[2] // 3
    segments = segment_ids[0]
    live_rows = padding[0]
    stream = patches[0]
    gathered = lax.all_gather(stream, "grp", axis=0, tiled=True)
    normed = normalize(gathered.astype(jnp.float32), first_gain, first_shift).astype(jnp.bfloat16)
    lifted = jnp.einsum("sd,dhe->she", normed, input_weight, preferred_element_type=jnp.float32)
    projected = (lifted + input_shift[None]).astype(jnp.bfloat16)
    mixed = attend(projected, segments, live_rows, head_dim)
    block = lax.optimization_barrier(mixed)
    attended = summed_apart(
        jnp.einsum("qhe,hed->qd", block, output_weight, preferred_element_type=jnp.float32).astype(
            jnp.bfloat16
        )
    )
    residual = (stream.astype(jnp.float32) + attended + output_shift).astype(jnp.bfloat16)
    normed_again = normalize(residual.astype(jnp.float32), second_gain, second_shift).astype(
        jnp.bfloat16
    )
    lifted = (
        jnp.dot(
            lax.all_gather(normed_again, "grp", axis=0, tiled=True),
            up_weight,
            preferred_element_type=jnp.float32,
        )
        + up_shift
    )
    activated = jax.nn.gelu(lifted, approximate=False).astype(jnp.bfloat16)
    block = lax.optimization_barrier(activated)
    fed = summed_apart(
        jnp.dot(block, down_weight, preferred_element_type=jnp.float32).astype(jnp.bfloat16)
    )
    layer_out = (residual.astype(jnp.float32) + fed + down_shift).astype(jnp.bfloat16)
    windows = layer_out.reshape(row_count // 4, 4 * model_width)
    merged = (
        jnp.dot(
            lax.all_gather(windows, "grp", axis=0, tiled=True),
            merge_weight,
            preferred_element_type=jnp.float32,
        )
        + merge_shift
    ).astype(jnp.bfloat16)
    outgoing = routed_rows(merged, segments, live_rows, request_owner[0])
    delivered = lax.all_to_all(outgoing, "tok", split_axis=0, concat_axis=0, tiled=True)
    return delivered[None]


def solution(mesh):
    return jax.shard_map(
        on_device,
        mesh=mesh,
        in_specs=(
            P("tok", "grp", None),
            P("tok", None),
            P("tok", None),
            P("tok", None),
            P(),
            P(),
            P(None, "grp", None),
            P("grp", None),
            P("grp", None, None),
            P(),
            P(),
            P(),
            P(None, "grp"),
            P("grp"),
            P("grp", None),
            P(),
            P(None, "grp"),
            P("grp"),
        ),
        out_specs=P("tok", None, None, "grp"),
        check_vma=False,
    )
```

profile of v0, /device:TPU:1, one launch (start us, length us, event | category | flops | bytes accessed | tf_op | source)
XLA Modules:
  0.0 143.6 jit_solution(7038068006779687679)
XLA Ops:
  0.0 27.2 %all-gather = bf16[1,256,1664]{2,1,0:T(8,128)(2,1)S(1)} all-gather(bf16[1,16,1664]{2,1,0:T(8,128)(2,1)} %param.18), channel_id=2, replica_groups=mesh['grp'=16,'tok'=32] {'grp'}, dimensions={1}, use_global_device_ids=true | all-gather | bytes 905216 | tf_op jit(solution)/shard_map/all_gather | solution.py:102
  27.2 0.2 convert_reduce_fusion
  27.5 0.4 fusion.3
  27.9 0.7 fusion.9
  28.6 0.3 fusion.50
  28.9 0.2 fusion.30
  29.1 0.1 fusion.32
  29.2 0.2 fusion.10
  29.4 0.2 copy-done.3
  29.6 0.4 convolution_convert_fusion.1
  30.1 27.0 %all_to_all.15 = bf16[16,16,1664]{2,1,0:T(8,128)(2,1)S(1)} all-to-all(bf16[16,16,1664]{2,1,0:T(8,128)(2,1)S(1)} %bitcast.72), channel_id=1, replica_groups=mesh['grp'=16,'tok'=32] {'grp'}, dimensions={0} | all-to-all | bytes 1703936 | tf_op jit(solution)/shard_map/all_to_all | solution.py:50
  57.1 0.1 convert_reduce_fusion.2
  57.3 0.1 convert_reduce_fusion.3
  57.4 0.2 fusion.35
  57.7 0.1 fusion.38
  57.7 16.8 %all_gather.10 = bf16[256,1664]{1,0:T(8,128)(2,1)S(1)} all-gather(bf16[16,1664]{1,0:T(8,128)(2,1)S(1)} %fusion.38), channel_id=1, replica_groups=mesh['grp'=16,'tok'=32] {'grp'}, dimensions={0}, use_global_device_ids=true | all-gather | bytes 905216 | tf_op jit(solution)/shard_map/all_gather | solution.py:119
  74.6 1.0 fusion.21
  75.6 0.2 copy-done.1
  75.7 1.4 convolution_convert_fusion
  77.1 5.3 %all-to-all-start.1 = ((bf16[16,16,1664]{2,1,0:T(8,128)(2,1)}), bf16[16,16,1664]{2,1,0:T(8,128)(2,1)S(1)}, u32[]{:S(2)}, u32[]{:S(2)}) async-start(bf16[16,16,1664]{2,1,0:T(8,128)(2,1)} %bitcast.17), calls=%async_computation.1 | async-start | bytes 1703936 | tf_op jit(solution)/shard_map/all_to_all | solution.py:50
  82.4 0.2 slice.15
  82.7 0.2 slice.16
  82.8 0.2 convert_reduce_fusion.4
  83.0 0.1 select_reduce_fusion
  83.2 23.3 %all-to-all-done.1 = bf16[16,16,1664]{2,1,0:T(8,128)(2,1)S(1)} async-done(((bf16[16,16,1664]{2,1,0:T(8,128)(2,1)}), bf16[16,16,1664]{2,1,0:T(8,128)(2,1)S(1)}, u32[]{:S(2)}, u32[]{:S(2)}) %all-to-all-start.1) | async-done | bytes 852000 | tf_op jit(solution)/shard_map/all_to_all | solution.py:50
  106.4 0.1 convert_reduce_fusion.1
  106.7 16.8 %all-gather.1 = bf16[16,4,6656]{2,1,0:T(4,128)(2,1)S(1)} all-gather(bf16[1,4,6656]{2,1,0:T(4,128)(2,1)S(1)} %fusion.43), channel_id=1, replica_groups=mesh['grp'=16,'tok'=32] {'grp'}, dimensions={0}, use_global_device_ids=true | all-gather | bytes 905216 | tf_op jit(solution)/shard_map/all_gather | solution.py:134
  123.5 0.2 reshape.122
  123.7 0.8 convolution_convert_fusion.2
  124.5 0.1 copy.26
  124.7 18.3 %all_to_all.16 = bf16[32,8,104]{2,1,0:T(8,128)(2,1)S(1)} all-to-all(bf16[32,8,104]{2,1,0:T(8,128)(2,1)S(1)} %bitcast.73), channel_id=1, replica_groups=mesh['grp'=16,'tok'=32] {'tok'}, dimensions={0} | all-to-all | bytes 106496 | tf_op jit(solution)/shard_map/all_to_all | solution.py:141
  143.0 0.6 copy.29
  (50 shorter events, 0.4 us)
Async XLA Ops:
  0.0 123.7 %copy-start = (bf16[6656,104]{0,1:T(8,128)(2,1)S(1)}, bf16[6656,104]{0,1:T(8,128)(2,1)}, u32[]{:S(2)}) copy-start(bf16[6656,104]{0,1:T(8,128)(2,1)} %param.34) | copy-start | bytes 4153348
  0.0 27.8 %copy-start.16 = (s32[1,256]{1,0:T(1,128)S(1)}, s32[1,256]{1,0:T(1,128)}, u32[]{:S(2)}) copy-start(s32[1,256]{1,0:T(1,128)} %param.20) | copy-start | bytes 3076
  0.0 27.9 %copy-start.9 = (f32[1,312]{1,0:T(1,128)S(1)}, f32[1,312]{1,0:T(1,128)}, u32[]{:S(2)}) copy-start(f32[1,312]{1,0:T(1,128)} %param.25) | copy-start | bytes 3748
  0.0 27.9 %copy-start.14 = (f32[1664]{0:T(1024)S(1)}, f32[1664]{0:T(1024)}, u32[]{:S(2)}) copy-start(f32[1664]{0:T(1024)} %param.22) | copy-start | bytes 19972
  0.0 27.9 %copy-start.13 = (f32[1664]{0:T(1024)S(1)}, f32[1664]{0:T(1024)}, u32[]{:S(2)}) copy-start(f32[1664]{0:T(1024)} %param.23) | copy-start | bytes 19972
  0.0 27.9 %copy-start.11 = (bf16[1664,1,312]{0,2,1:T(8,128)(2,1)S(1)}, bf16[1664,1,312]{0,2,1:T(8,128)(2,1)}, u32[]{:S(2)}) copy-start(bf16[1664,1,312]{0,2,1:T(8,128)(2,1)} %param.24) | copy-start | bytes 3115012
  27.9 0.7 copy-start.5
  28.6 1.0 copy-start.3
  30.0 27.2 %copy-start.2 = (bf16[1,16,1664]{2,1,0:T(8,128)(2,1)S(1)}, bf16[1,16,1664]{2,1,0:T(8,128)(2,1)}, u32[]{:S(2)}) copy-start(bf16[1,16,1664]{2,1,0:T(8,128)(2,1)} %param.18) | copy-start | bytes 159748
  30.1 27.2 %copy-start.4 = (f32[1664]{0:T(1024)S(1)}, f32[1664]{0:T(1024)}, u32[]{:S(2)}) copy-start(f32[1664]{0:T(1024)} %param.27) | copy-start | bytes 19972
  30.1 27.6 %copy-start.7 = (f32[1664]{0:T(1024)S(1)}, f32[1664]{0:T(1024)}, u32[]{:S(2)}) copy-start(f32[1664]{0:T(1024)} %param.29) | copy-start | bytes 19972
  30.1 27.6 %copy-start.8 = (f32[1664]{0:T(1024)S(1)}, f32[1664]{0:T(1024)}, u32[]{:S(2)}) copy-start(f32[1664]{0:T(1024)} %param.28) | copy-start | bytes 19972
  57.1 17.4 %copy-start.12 = (bf16[1664,256]{1,0:T(8,128)(2,1)S(1)}, bf16[1664,256]{1,0:T(8,128)(2,1)}, u32[]{:S(2)}) copy-start(bf16[1664,256]{1,0:T(8,128)(2,1)} %param.30) | copy-start | bytes 2555908
  57.1 17.4 %copy-start.15 = (f32[256]{0:T(256)S(1)}, f32[256]{0:T(256)}, u32[]{:S(2)}) copy-start(f32[256]{0:T(256)} %param.31) | copy-start | bytes 3076
  74.6 1.2 copy-start.1
  77.1 5.6 %copy-start.6 = (f32[1664]{0:T(1024)S(1)}, f32[1664]{0:T(1024)}, u32[]{:S(2)}) copy-start(f32[1664]{0:T(1024)} %param.33) | copy-start | bytes 19972
  77.1 5.9 %copy-start.17 = (s32[1,32]{1,0:T(1,128)S(1)}, s32[1,32]{1,0:T(1,128)}, u32[]{:S(2)}) copy-start(s32[1,32]{1,0:T(1,128)} %param.21) | copy-start | bytes 388
  77.1 29.4 %all-to-all-start.1 = ((bf16[16,16,1664]{2,1,0:T(8,128)(2,1)}), bf16[16,16,1664]{2,1,0:T(8,128)(2,1)S(1)}, u32[]{:S(2)}, u32[]{:S(2)}) async-start(bf16[16,16,1664]{2,1,0:T(8,128)(2,1)} %bitcast.17), calls=%async_computation.1 | async-start | bytes 1703936 | tf_op jit(solution)/shard_map/all_to_all | solution.py:50
  106.7 17.0 %copy-start.10 = (f32[104]{0:T(128)S(1)}, f32[104]{0:T(128)}, u32[]{:S(2)}) copy-start(f32[104]{0:T(128)} %param.35) | copy-start | bytes 1252
where the time goes:
time: 144 us
  blocking collectives  106 us (74%)
  waiting for transfers between devices  23.3 us (16%)
  starting transfers between devices  5.33 us (4%)
  matrix products  4.68 us (3%)
  other arithmetic  1.96 us (1%)
  local copies, waits for them, and re-layouts  1.85 us (1%)
    all_gather x1, blocking collectives, on_device(): gathered = lax.all_gather(stream, 'grp', axis=0, tiled=True)  27.2 us
    all_to_all x1, blocking collectives, summed_apart(): lax.all_to_all(terms.reshape(shards, rows, terms.shape[1]), 'grp', 0, 0,...  27 us
    all_to_all x1, waiting for transfers between devices, summed_apart(): lax.all_to_all(terms.reshape(shards, rows, terms.shape[1]), 'grp', 0, 0,...  23.3 us
    all_to_all x1, blocking collectives, on_device(): lax.all_to_all(outgoing, 'tok', split_axis=0, concat_axis=0, tiled=True)  18.3 us
    all_gather x1, blocking collectives, on_device(): lax.all_gather(windows, 'grp', axis=0, tiled=True)  16.8 us
    all_gather x1, blocking collectives, on_device(): lax.all_gather(normed_again, 'grp', axis=0, tiled=True)  16.8 us
    all_to_all x1, starting transfers between devices, summed_apart(): lax.all_to_all(terms.reshape(shards, rows, terms.shape[1]), 'grp', 0, 0,...  5.33 us
  transfers between devices with their start and end apart: 1, of which 1 were waited for; matrix products, arithmetic and copies ran while one was open for 0% of the time, Pallas kernels for 0%

commit v1 on v0

--- a/solution.py
+++ b/solution.py
@@ -131,7 +131,9 @@
     windows = layer_out.reshape(row_count // 4, 4 * model_width)
     merged = (
         jnp.dot(
-            lax.all_gather(windows, "grp", axis=0, tiled=True),
+            jnp.concatenate(
+                lax.all_to_all(jnp.stack([windows] * lax.axis_size("grp")), "grp", 0, 0), axis=0
+            ),
             merge_weight,
             preferred_element_type=jnp.float32,
         )

time: 144 us -> 156 us (1.083)
  waiting for transfers between devices: 23.3 us -> 46.9 us
  blocking collectives: 106 us -> 89.4 us
  starting transfers between devices: 5.33 us -> 8.98 us
    all_to_all x0 -> x1, waiting for transfers between devices: none -> 23 us  [on_device(): lax.all_to_all(jnp.stack([windows] * lax.axis_size('grp')), 'grp', 0, 0)]
    all_gather x1 -> x0, blocking collectives: 16.8 us -> none  [on_device(): lax.all_gather(windows, 'grp', axis=0, tiled=True)]
    all_to_all x0 -> x1, starting transfers between devices: none -> 3.65 us  [on_device(): lax.all_to_all(jnp.stack([windows] * lax.axis_size('grp')), 'grp', 0, 0)]
  transfers between devices with their start and end apart: 1 -> 2, of which waited for: 1 -> 2; matrix products, arithmetic and copies ran while one was open for 0% -> 0% of each run, Pallas kernels for 0% -> 0%
where the time goes in v1:
time: 156 us; the launch traced here: 155 us
  blocking collectives  89.4 us (57%)
  waiting for transfers between devices  46.9 us (30%)
  starting transfers between devices  8.98 us (6%)
  matrix products  4.68 us (3%)
  local copies, waits for them, and re-layouts  2.99 us (2%)
  other arithmetic  1.95 us (1%)
    all_gather x1, blocking collectives, on_device(): gathered = lax.all_gather(stream, 'grp', axis=0, tiled=True)  27.2 us
    all_to_all x1, blocking collectives, summed_apart(): lax.all_to_all(terms.reshape(shards, rows, terms.shape[1]), 'grp', 0, 0,...  27 us
    all_to_all x1, waiting for transfers between devices, summed_apart(): lax.all_to_all(terms.reshape(shards, rows, terms.shape[1]), 'grp', 0, 0,...  23.9 us
    all_to_all x1, waiting for transfers between devices, on_device(): lax.all_to_all(jnp.stack([windows] * lax.axis_size('grp')), 'grp', 0, 0)  23 us
    all_to_all x1, blocking collectives, on_device(): lax.all_to_all(outgoing, 'tok', split_axis=0, concat_axis=0, tiled=True)  18.3 us
    all_gather x1, blocking collectives, on_device(): lax.all_gather(normed_again, 'grp', axis=0, tiled=True)  16.8 us
    all_to_all x1, starting transfers between devices, summed_apart(): lax.all_to_all(terms.reshape(shards, rows, terms.shape[1]), 'grp', 0, 0,...  5.33 us
    all_to_all x1, starting transfers between devices, on_device(): lax.all_to_all(jnp.stack([windows] * lax.axis_size('grp')), 'grp', 0, 0)  3.65 us
  transfers between devices with their start and end apart: 2, of which 2 were waited for; matrix products, arithmetic and copies ran while one was open for 0% of the time, Pallas kernels for 0%

profile of v1, /device:TPU:1, one launch (start us, length us, event | category | flops | bytes accessed | tf_op | source)
XLA Modules:
  0.0 155.2 jit_solution(5410796431067598895)
XLA Ops:
  0.0 27.2 %all-gather = bf16[1,256,1664]{2,1,0:T(8,128)(2,1)S(1)} all-gather(bf16[1,16,1664]{2,1,0:T(8,128)(2,1)} %param.18), channel_id=2, replica_groups=mesh['grp'=16,'tok'=32] {'grp'}, dimensions={1}, use_global_device_ids=true | all-gather | bytes 905216 | tf_op jit(solution)/shard_map/all_gather | solution.py:102
  27.2 0.2 convert_reduce_fusion
  27.5 0.4 fusion.3
  27.9 0.7 fusion.9
  28.6 0.3 fusion.49
  28.9 0.2 fusion.30
  29.1 0.1 fusion.32
  29.2 0.2 fusion.10
  29.4 0.2 copy-done.3
  29.6 0.4 convolution_convert_fusion.1
  30.1 27.0 %all_to_all.20 = bf16[16,16,1664]{2,1,0:T(8,128)(2,1)S(1)} all-to-all(bf16[16,16,1664]{2,1,0:T(8,128)(2,1)S(1)} %bitcast.70), channel_id=1, replica_groups=mesh['grp'=16,'tok'=32] {'grp'}, dimensions={0} | all-to-all | bytes 1703936 | tf_op jit(solution)/shard_map/all_to_all | solution.py:50
  57.1 0.1 convert_reduce_fusion.2
  57.3 0.1 convert_reduce_fusion.3
  57.4 0.2 fusion.35
  57.7 16.8 %all_gather.7 = bf16[256,1664]{1,0:T(8,128)(2,1)S(1)} all-gather(bf16[16,1664]{1,0:T(8,128)(2,1)S(1)} %fusion.38), channel_id=1, replica_groups=mesh['grp'=16,'tok'=32] {'grp'}, dimensions={0}, use_global_device_ids=true | all-gather | bytes 905216 | tf_op jit(solution)/shard_map/all_gather | solution.py:119
  74.6 1.0 fusion.21
  75.6 0.2 copy-done.1
  75.7 1.3 convolution_convert_fusion
  77.1 5.3 %all-to-all-start.1 = ((bf16[16,16,1664]{2,1,0:T(8,128)(2,1)}), bf16[16,16,1664]{2,1,0:T(8,128)(2,1)S(1)}, u32[]{:S(2)}, u32[]{:S(2)}) async-start(bf16[16,16,1664]{2,1,0:T(8,128)(2,1)} %bitcast.17), calls=%async_computation.1 | async-start | bytes 1703936 | tf_op jit(solution)/shard_map/all_to_all | solution.py:50
  82.6 23.9 %all-to-all-done.1 = bf16[16,16,1664]{2,1,0:T(8,128)(2,1)S(1)} async-done(((bf16[16,16,1664]{2,1,0:T(8,128)(2,1)}), bf16[16,16,1664]{2,1,0:T(8,128)(2,1)S(1)}, u32[]{:S(2)}, u32[]{:S(2)}) %all-to-all-start.1) | async-done | bytes 852000 | tf_op jit(solution)/shard_map/all_to_all | solution.py:50
  106.4 0.1 convert_reduce_fusion.1
  106.7 1.1 stack.3
  107.8 3.7 %all-to-all-start.2 = ((bf16[16,4,6656]{2,1,0:T(4,128)(2,1)}), bf16[16,4,6656]{2,1,0:T(4,128)(2,1)S(1)}, u32[]{:S(2)}, u32[]{:S(2)}) async-start(bf16[16,4,6656]{2,1,0:T(4,128)(2,1)} %stack.3), calls=%async_computation.2 | async-start | bytes 1703936 | tf_op jit(solution)/shard_map/all_to_all | solution.py:135
  111.5 0.2 slice.15
  111.6 0.2 slice.16
  111.8 0.2 convert_reduce_fusion.4
  112.1 23.0 %all-to-all-done.2 = bf16[16,4,6656]{2,1,0:T(4,128)(2,1)S(1)} async-done(((bf16[16,4,6656]{2,1,0:T(4,128)(2,1)}), bf16[16,4,6656]{2,1,0:T(4,128)(2,1)S(1)}, u32[]{:S(2)}, u32[]{:S(2)}) %all-to-all-start.2) | async-done | bytes 852000 | tf_op jit(solution)/shard_map/all_to_all | solution.py:135
  135.1 0.2 reshape.122
  135.3 0.8 convolution_convert_fusion.2
  136.1 0.1 copy.24
  136.3 18.3 %all_to_all.21 = bf16[32,8,104]{2,1,0:T(8,128)(2,1)S(1)} all-to-all(bf16[32,8,104]{2,1,0:T(8,128)(2,1)S(1)} %bitcast.71), channel_id=1, replica_groups=mesh['grp'=16,'tok'=32] {'tok'}, dimensions={0} | all-to-all | bytes 106496 | tf_op jit(solution)/shard_map/all_to_all | solution.py:143
  154.5 0.6 copy.27
  (52 shorter events, 0.6 us)
Async XLA Ops:
  0.0 135.3 %copy-start = (bf16[6656,104]{0,1:T(8,128)(2,1)S(1)}, bf16[6656,104]{0,1:T(8,128)(2,1)}, u32[]{:S(2)}) copy-start(bf16[6656,104]{0,1:T(8,128)(2,1)} %param.34) | copy-start | bytes 4153348
  0.0 27.8 %copy-start.16 = (s32[1,256]{1,0:T(1,128)S(1)}, s32[1,256]{1,0:T(1,128)}, u32[]{:S(2)}) copy-start(s32[1,256]{1,0:T(1,128)} %param.20) | copy-start | bytes 3076
  0.0 27.9 %copy-start.9 = (f32[1,312]{1,0:T(1,128)S(1)}, f32[1,312]{1,0:T(1,128)}, u32[]{:S(2)}) copy-start(f32[1,312]{1,0:T(1,128)} %param.25) | copy-start | bytes 3748
  0.0 27.9 %copy-start.14 = (f32[1664]{0:T(1024)S(1)}, f32[1664]{0:T(1024)}, u32[]{:S(2)}) copy-start(f32[1664]{0:T(1024)} %param.22) | copy-start | bytes 19972
  0.0 27.9 %copy-start.13 = (f32[1664]{0:T(1024)S(1)}, f32[1664]{0:T(1024)}, u32[]{:S(2)}) copy-start(f32[1664]{0:T(1024)} %param.23) | copy-start | bytes 19972
  0.0 27.9 %copy-start.11 = (bf16[1664,1,312]{0,2,1:T(8,128)(2,1)S(1)}, bf16[1664,1,312]{0,2,1:T(8,128)(2,1)}, u32[]{:S(2)}) copy-start(bf16[1664,1,312]{0,2,1:T(8,128)(2,1)} %param.24) | copy-start | bytes 3115012
  27.9 0.7 copy-start.5
  28.6 1.0 copy-start.3
  30.0 27.2 %copy-start.2 = (bf16[1,16,1664]{2,1,0:T(8,128)(2,1)S(1)}, bf16[1,16,1664]{2,1,0:T(8,128)(2,1)}, u32[]{:S(2)}) copy-start(bf16[1,16,1664]{2,1,0:T(8,128)(2,1)} %param.18) | copy-start | bytes 159748
  30.1 27.2 %copy-start.4 = (f32[1664]{0:T(1024)S(1)}, f32[1664]{0:T(1024)}, u32[]{:S(2)}) copy-start(f32[1664]{0:T(1024)} %param.27) | copy-start | bytes 19972
  30.1 27.6 %copy-start.7 = (f32[1664]{0:T(1024)S(1)}, f32[1664]{0:T(1024)}, u32[]{:S(2)}) copy-start(f32[1664]{0:T(1024)} %param.29) | copy-start | bytes 19972
  30.1 27.6 %copy-start.8 = (f32[1664]{0:T(1024)S(1)}, f32[1664]{0:T(1024)}, u32[]{:S(2)}) copy-start(f32[1664]{0:T(1024)} %param.28) | copy-start | bytes 19972
  57.1 17.4 %copy-start.12 = (bf16[1664,256]{1,0:T(8,128)(2,1)S(1)}, bf16[1664,256]{1,0:T(8,128)(2,1)}, u32[]{:S(2)}) copy-start(bf16[1664,256]{1,0:T(8,128)(2,1)} %param.30) | copy-start | bytes 2555908
  57.1 17.4 %copy-start.15 = (f32[256]{0:T(256)S(1)}, f32[256]{0:T(256)}, u32[]{:S(2)}) copy-start(f32[256]{0:T(256)} %param.31) | copy-start | bytes 3076
  74.6 1.2 copy-start.1
  77.1 5.4 %copy-start.6 = (f32[1664]{0:T(1024)S(1)}, f32[1664]{0:T(1024)}, u32[]{:S(2)}) copy-start(f32[1664]{0:T(1024)} %param.33) | copy-start | bytes 19972
  77.1 29.4 %all-to-all-start.1 = ((bf16[16,16,1664]{2,1,0:T(8,128)(2,1)}), bf16[16,16,1664]{2,1,0:T(8,128)(2,1)S(1)}, u32[]{:S(2)}, u32[]{:S(2)}) async-start(bf16[16,16,1664]{2,1,0:T(8,128)(2,1)} %bitcast.17), calls=%async_computation.1 | async-start | bytes 1703936 | tf_op jit(solution)/shard_map/all_to_all | solution.py:50
  106.7 5.3 %copy-start.17 = (s32[1,32]{1,0:T(1,128)S(1)}, s32[1,32]{1,0:T(1,128)}, u32[]{:S(2)}) copy-start(s32[1,32]{1,0:T(1,128)} %param.21) | copy-start | bytes 388
  107.8 27.5 %copy-start.10 = (f32[104]{0:T(128)S(1)}, f32[104]{0:T(128)}, u32[]{:S(2)}) copy-start(f32[104]{0:T(128)} %param.35) | copy-start | bytes 1252
  107.8 27.3 %all-to-all-start.2 = ((bf16[16,4,6656]{2,1,0:T(4,128)(2,1)}), bf16[16,4,6656]{2,1,0:T(4,128)(2,1)S(1)}, u32[]{:S(2)}, u32[]{:S(2)}) async-start(bf16[16,4,6656]{2,1,0:T(4,128)(2,1)} %stack.3), calls=%async_computation.2 | async-start | bytes 1703936 | tf_op jit(solution)/shard_map/all_to_all | solution.py:135
